TPU v7x, 32 devices: a whole 2x2x4 slice. The times are simulated.
32 devices in a mesh: ctx: 8 (over z, y), tp: 4 (over x, core).
Axes of the slice: x: 2, y: 2, z: 4, core: 2. Of those that a mesh axis runs over, the one named last changes fastest.
Arguments:
- tokens: bfloat16 [1024, 4096], P('ctx'), may hold values from -6 to 6
- w_query: bfloat16 [4096, 2048], P('ctx', 'tp'), may hold values from -0.09375 to 0.09375
- w_key: bfloat16 [4096, 2048], P('ctx', 'tp'), may hold values from -0.09375 to 0.09375
- w_value: bfloat16 [4096, 2048], P('ctx', 'tp'), may hold values from -0.09375 to 0.09375
- taps_query: float32 [3, 2048], P(None, 'tp'), may hold values from -3.5 to 3.5
- taps_key: float32 [3, 2048], P(None, 'tp'), may hold values from -3.5 to 3.5
- taps_value: float32 [3, 2048], P(None, 'tp'), may hold values from -3.5 to 3.5
- decay_rate: float32 [16, 2048], P(None, 'tp'), may hold values from 1e-05 to 0.03
- residue: float32 [16, 2048], P(None, 'tp'), may hold values from -1.5 to 1.5
- skip_gain: float32 [2048], P('tp'), may hold values from -3 to 3
- w_out: bfloat16 [2048, 4096], P('ctx', 'tp'), may hold values from -0.125 to 0.125
Outputs:
- layer_out: bfloat16 [1024, 4096], P('ctx', 'tp')
All inputs are finite; a program needn't handle non-finite values.
Results may differ from a plain program's by a relative error of at most 0.015.
Values may be sent and summed in bfloat16 or wider, within the bound.
No kernel may reach another device: no remote copies, remote signals or barrier semaphores. Data moves between devices by JAX's collectives and lax.ppermute only.
A program may use at most 128 MiB of HBM per device.

v0:
```python
import jax
import jax.numpy as jnp
from jax import lax
from jax.sharding import PartitionSpec as P


def short_conv(padded, taps):
    return taps[0] * padded[2:] + taps[1] * padded[1:-1] + taps[2] * padded[:-2]


def modal_long_conv(signal, rates, residues, skips):
    length, width = signal.shape
    order = rates.shape[0]
    ctx_count = lax.axis_size("ctx")
    me = lax.axis_index("ctx")
    coefs = residues * jnp.sqrt(2.0 * rates)
    times = jnp.arange(length, dtype=jnp.float32)[:, None, None]
    grow = jnp.exp(rates[None] * times)
    decay = jnp.exp(-rates[None] * times)
    lifted = (grow * signal[:, None, :]).reshape(length, order * width)
    rows = jnp.arange(length, dtype=jnp.int32)
    lower = (rows[:, None] >= rows[None, :]).astype(jnp.float32)
    running = jnp.matmul(lower, lifted, precision=lax.Precision.HIGHEST).reshape(
        length, order, width
    )
    end_state = running[length - 1] * jnp.exp(-rates * (length - 1))
    states = lax.all_gather(end_state, "ctx", axis=0, tiled=False)
    chunk_ids = jnp.arange(ctx_count, dtype=jnp.int32)
    gap = jnp.maximum(me - 1 - chunk_ids, 0).astype(jnp.float32)
    carry_w = jnp.where(
        (chunk_ids < me)[:, None, None], jnp.exp(-rates[None] * (gap[:, None, None] * length)), 0.0
    )
    carried = jnp.sum(carry_w * states, axis=0) * jnp.exp(-rates)
    total = running + carried[None]
    mixed = jnp.sum(coefs[None] * decay * total, axis=1)
    return mixed + skips * signal


def body(
    tokens,
    w_query,
    w_key,
    w_value,
    taps_query,
    taps_key,
    taps_value,
    decay_rate,
    residue,
    skip_gain,
    w_out,
):
    ctx_count = lax.axis_size("ctx")
    halo = lax.ppermute(tokens[-2:], "ctx", perm=[(i, i + 1) for i in range(ctx_count - 1)])
    rows = jnp.concatenate([halo, tokens], axis=0)

    def project(piece):
        full = lax.all_gather(piece, "ctx", axis=0, tiled=True)
        out = jnp.dot(rows, full, preferred_element_type=jnp.float32)
        return out.astype(jnp.bfloat16).astype(jnp.float32)

    queries = project(w_query)
    keys_proj = project(w_key)
    values_proj = project(w_value)
    gate = short_conv(queries, taps_query).astype(jnp.bfloat16)
    product = (short_conv(keys_proj, taps_key) * short_conv(values_proj, taps_value)).astype(
        jnp.bfloat16
    )
    mixed = modal_long_conv(product.astype(jnp.float32), decay_rate, residue, skip_gain)
    mixed = mixed.astype(jnp.bfloat16)
    gated = (gate.astype(jnp.float32) * mixed.astype(jnp.float32)).astype(jnp.bfloat16)
    features = lax.all_gather(gated, "tp", axis=1, tiled=True)
    result = jnp.dot(
        features,
        lax.all_gather(w_out, "ctx", axis=0, tiled=True),
        preferred_element_type=jnp.float32,
    )
    return result.astype(jnp.bfloat16)


def solution(mesh):
    in_specs = (
        P("ctx", None),
        P("ctx", "tp"),
        P("ctx", "tp"),
        P("ctx", "tp"),
        P(None, "tp"),
        P(None, "tp"),
        P(None, "tp"),
        P(None, "tp"),
        P(None, "tp"),
        P("tp"),
        P("ctx", "tp"),
    )
    out_specs = P("ctx", "tp")
    return jax.shard_map(body, mesh=mesh, in_specs=in_specs, out_specs=out_specs, check_vma=False)
```

profile of v0, /device:TPU:0, one launch (start us, length us, event | category | flops | bytes accessed | tf_op | source)
XLA Modules:
  0.0 319.4 jit_solution(1594210370774384721)
XLA Ops:
  6.5 0.0 copy-start.4
  6.5 0.0 all-gather.10.cloned.1.call-start
  6.5 0.7 all-gather.10.cloned.1.call-update
  7.3 0.0 all-gather.8.cloned.1.call-start
  7.3 0.7 all-gather.8.cloned.1.call-update
  8.0 0.0 all-gather.6.cloned.1.call-start
  8.1 0.7 all-gather.6.cloned.1.call-update
  8.7 0.0 all-gather.12.cloned.1.call-start
  8.8 0.5 all-gather.12.cloned.1.call-update
  9.3 0.9 slice.62
  10.2 4.9 %collective-permute-start = (bf16[2,4096]{1,0:T(2,128)(2,1)S(1)}, bf16[2,4096]{1,0:T(2,128)(2,1)S(1)}, u32[]{:S(2)}, u32[]{:S(2)}) collective-permute-start(bf16[2,4096]{1,0:T(2,128)(2,1)S(1)} %slice.62), channel_id=1, source_target_pairs={{0,4},{4,8},{8,12},{12,16},{16,20},{20,24},{24,28},{1,5},{5,9},{9,... | collective-permute-start | bytes 49160 | tf_op jit(solution)/shard_map/ppermute | solution.py:53
  15.1 0.8 fusion.26
  15.9 0.8 fusion.25
  16.7 0.8 fusion.24
  17.5 0.8 copy.12
  18.3 0.0 collective-permute-done
  18.3 67.3 %all-gather.10.cloned.1.call-done = bf16[4096,512]{1,0:T(8,128)(2,1)} async-done(((bf16[512,512]{1,0:T(8,128)(2,1)}), bf16[4096,512]{1,0:T(8,128)(2,1)}) %all-gather.10.cloned.1.call-update) | async-done | bytes 4194320 | tf_op jit(solution)/shard_map/all_gather | solution.py:57
  85.6 3.3 %fusion.8 = f32[130,512]{1,0:T(8,128)S(1)} fusion(bf16[4096,512]{1,0:T(8,128)(2,1)} %all-gather.10.cloned.1.call-done, bf16[128,4096]{1,0:T(8,128)(2,1)} %param.11, bf16[2,4096]{1,0:T(2,128)(2,1)S(1)} %collective-permute-done), kind=kOutput, calls=%fused_computation.11 | convolution fusion | flops 547522560 | bytes 5525504 | tf_op jit(solution)/shard_map/dot_general | solution.py:58
  88.9 70.5 %all-gather.8.cloned.1.call-done = bf16[4096,512]{1,0:T(8,128)(2,1)} async-done(((bf16[512,512]{1,0:T(8,128)(2,1)}), bf16[4096,512]{1,0:T(8,128)(2,1)}) %all-gather.8.cloned.1.call-update) | async-done | bytes 4194320 | tf_op jit(solution)/shard_map/all_gather | solution.py:57
  159.4 0.0 copy-done.4
  159.4 2.9 fusion.9
  162.4 0.2 fusion.20
  162.6 0.5 mul.240
  163.1 3.4 %copy.13 = f32[16,8,16,512]{3,1,2,0:T(8,128)S(1)} copy(f32[16,8,16,512]{3,2,1,0:T(8,128)S(1)} %bitcast.28) | data formatting | bytes 8388608
  166.5 2.9 fusion.2
  169.4 0.0 copy-start.1
  169.5 0.0 copy-start.2
  169.5 5.2 %copy.14 = f32[16,8,16,512]{3,2,1,0:T(8,128)} copy(f32[16,8,16,512]{3,1,2,0:T(8,128)S(1)} %bitcast.26) | data formatting | bytes 8388608
  174.7 0.1 slice_reduce_fusion
  174.8 0.0 copy-done.1
  174.8 0.0 copy-done.2
  174.9 31.8 %all-gather = f32[128,512]{1,0:T(8,128)S(1)} all-gather(f32[16,512]{1,0:T(8,128)S(1)} %get-tuple-element.6), channel_id=2, replica_groups=mesh['ctx'=8,'tp'=4] {'ctx'}, dimensions={0}, use_global_device_ids=true | all-gather | bytes 294912 | tf_op jit(solution)/shard_map/all_gather | solution.py:27
  206.7 0.1 multiply_reduce_fusion
  206.8 0.0 copy-start.3
  206.8 28.2 %all-gather.6.cloned.1.call-done = bf16[4096,512]{1,0:T(8,128)(2,1)} async-done(((bf16[512,512]{1,0:T(8,128)(2,1)}), bf16[4096,512]{1,0:T(8,128)(2,1)}) %all-gather.6.cloned.1.call-update) | async-done | bytes 4194320 | tf_op jit(solution)/shard_map/all_gather | solution.py:57
  235.0 0.0 copy-start
  235.0 3.1 fusion.10
  238.1 0.3 copy-done
  238.4 1.5 fusion.1
  239.9 0.0 copy-done.3
  239.9 0.1 multiply_convert_fusion
  240.1 7.2 %all_gather.26 = bf16[128,2048]{1,0:T(8,128)(2,1)S(1)} all-gather(bf16[128,512]{1,0:T(8,128)(2,1)S(1)} %multiply_convert_fusion), channel_id=1, replica_groups=mesh['ctx'=8,'tp'=4] {'tp'}, dimensions={1}, use_global_device_ids=true | all-gather | bytes 655360 | tf_op jit(solution)/shard_map/all_gather | solution.py:71
  247.2 62.0 %all-gather.12.cloned.1.call-done = bf16[2048,1024]{1,0:T(8,128)(2,1)} async-done(((bf16[256,1024]{1,0:T(8,128)(2,1)}), bf16[2048,1024]{1,0:T(8,128)(2,1)}) %all-gather.12.cloned.1.call-update) | async-done | bytes 4194320 | tf_op jit(solution)/shard_map/all_gather | solution.py:74
  309.2 3.6 %convolution_convert_fusion = bf16[128,1024]{1,0:T(8,128)(2,1)} fusion(bf16[128,2048]{1,0:T(8,128)(2,1)S(1)} %all_gather.26, bf16[2048,1024]{1,0:T(8,128)(2,1)} %all-gather.12.cloned.1.call-done), kind=kOutput, calls=%fused_computation.9 | convolution fusion | flops 537001984 | bytes 4980736 | tf_op jit(solution)/shard_map/dot_general | solution.py:72
  (5 shorter events, 0.1 us)
Async XLA Ops:
  6.5 152.9 %copy-start.4 = (bf16[128,4096]{1,0:T(8,128)(2,1)S(1)}, bf16[128,4096]{1,0:T(8,128)(2,1)}, u32[]{:S(2)}) copy-start(bf16[128,4096]{1,0:T(8,128)(2,1)} %param.11) | copy-start | bytes 3145732
  6.5 79.1 %all-gather.10.cloned.1.call-start = ((), (), s32[]{:S(2)}) async-start(), calls=%async_computation.2 | async-start | bytes 4718592 | tf_op jit(solution)/shard_map/all_gather | solution.py:57
  7.3 152.2 %all-gather.8.cloned.1.call-start = ((), (), s32[]{:S(2)}) async-start(), calls=%async_computation.1 | async-start | bytes 4718592 | tf_op jit(solution)/shard_map/all_gather | solution.py:57
  8.0 227.0 %all-gather.6.cloned.1.call-start = ((), (), s32[]{:S(2)}) async-start(), calls=%async_computation | async-start | bytes 4718592 | tf_op jit(solution)/shard_map/all_gather | solution.py:57
  8.7 300.5 %all-gather.12.cloned.1.call-start = ((), (), s32[]{:S(2)}) async-start(), calls=%async_computation.3 | async-start | bytes 4718592 | tf_op jit(solution)/shard_map/all_gather | solution.py:74
  10.2 8.1 %collective-permute-start = (bf16[2,4096]{1,0:T(2,128)(2,1)S(1)}, bf16[2,4096]{1,0:T(2,128)(2,1)S(1)}, u32[]{:S(2)}, u32[]{:S(2)}) collective-permute-start(bf16[2,4096]{1,0:T(2,128)(2,1)S(1)} %slice.62), channel_id=1, source_target_pairs={{0,4},{4,8},{8,12},{12,16},{16,20},{20,24},{24,28},{1,5},{5,9},{9,... | collective-permute-start | bytes 49160 | tf_op jit(solution)/shard_map/ppermute | solution.py:53
  169.4 5.4 %copy-start.1 = (f32[16,512]{1,0:T(8,128)S(1)}, f32[16,512]{1,0:T(8,128)}, u32[]{:S(2)}) copy-start(f32[16,512]{1,0:T(8,128)} %param.18) | copy-start | bytes 98308
  169.5 5.4 %copy-start.2 = (f32[16,512]{1,0:T(8,128)S(1)}, f32[16,512]{1,0:T(8,128)}, u32[]{:S(2)}) copy-start(f32[16,512]{1,0:T(8,128)} %param.19) | copy-start | bytes 98308
  206.8 33.1 %copy-start.3 = (f32[512]{0:T(512)S(1)}, f32[512]{0:T(512)}, u32[]{:S(2)}) copy-start(f32[512]{0:T(512)} %param.20) | copy-start | bytes 6148
  235.0 3.4 %copy-start = (f32[16,8,16,512]{3,2,1,0:T(8,128)S(1)}, f32[16,8,16,512]{3,2,1,0:T(8,128)}, u32[]{:S(2)}) copy-start(f32[16,8,16,512]{3,2,1,0:T(8,128)} %copy.14) | copy-start | bytes 12582916
Sparse Core Ops, SparseCore 0:
  9.5 76.0 all-gather.9
  87.7 71.6 all-gather.7
  161.6 73.3 all-gather.5
  237.0 72.2 all-gather.11
where the time goes:
time: 320 us; the launch traced here: 319 us
  waiting for transfers between devices  231 us (72%)
  blocking collectives  39 us (12%)
  matrix products  15.8 us (5%)
  local copies, waits for them, and re-layouts  13.7 us (4%)
  between operations  13.3 us (4%)
  starting transfers between devices  4.99 us (2%)
    all_gather x3, waiting for transfers between devices, project(): full = lax.all_gather(piece, 'ctx', axis=0, tiled=True)  166 us
    all_gather x1, waiting for transfers between devices, body(): lax.all_gather(w_out, 'ctx', axis=0, tiled=True)  62 us
    all_gather x1, blocking collectives, modal_long_conv(): states = lax.all_gather(end_state, 'ctx', axis=0, tiled=False)  31.8 us
    unnamed x13, local copies, waits for them, and re-layouts  9.79 us
    dot_general x3, matrix products, project(): out = jnp.dot(rows, full, preferred_element_type=jnp.float32)  9.3 us
    all_gather x1, blocking collectives, body(): features = lax.all_gather(gated, 'tp', axis=1, tiled=True)  7.19 us
  transfers between devices with their start and end apart: 5, of which 4 were waited for; matrix products, arithmetic and copies ran while one was open for 9% of the time, Pallas kernels for 0%

commit v1 on v0

--- a/solution.py
+++ b/solution.py
@@ -2,6 +2,20 @@
 import jax.numpy as jnp
 from jax import lax
 from jax.sharding import PartitionSpec as P
+
+
+def plan_the_panels(x_in, peer_axis):
+    ndev = jax.lax.axis_size(peer_axis)
+    crops = [(nth, (nth + 1) % ndev) for nth in range(ndev)]
+    seen = [(nth, (nth - 1) % ndev) for nth in range(ndev)]
+    tall, taken_in = ([x_in], [x_in])
+    for _ in range(ndev // 2):
+        tall.append(jax.lax.ppermute(tall[-1], peer_axis, crops))
+    for _ in range((ndev - 1) // 2):
+        taken_in.append(jax.lax.ppermute(taken_in[-1], peer_axis, seen))
+    arr_out = jnp.concatenate([*tall[::-1], *taken_in[1:]], 0)
+    found_now = jnp.roll(arr_out, (jax.lax.axis_index(peer_axis) - ndev // 2) * x_in.shape[0], 0)
+    return found_now
 
 
 def short_conv(padded, taps):
@@ -70,9 +84,7 @@
     gated = (gate.astype(jnp.float32) * mixed.astype(jnp.float32)).astype(jnp.bfloat16)
     features = lax.all_gather(gated, "tp", axis=1, tiled=True)
     result = jnp.dot(
-        features,
-        lax.all_gather(w_out, "ctx", axis=0, tiled=True),
-        preferred_element_type=jnp.float32,
+        features, plan_the_panels(w_out, peer_axis="ctx"), preferred_element_type=jnp.float32
     )
     return result.astype(jnp.bfloat16)
 

time: 320 us -> 308 us (0.963)
  waiting for transfers between devices: 231 us -> 190 us
  local copies, waits for them, and re-layouts: 13.7 us -> 29.2 us
  starting transfers between devices: 4.99 us -> 18.3 us
    ppermute x0 -> x7, waiting for transfers between devices: none -> 89.9 us  [the longest x4 78.3 us: plan_the_panels(): tall.append(jax.lax.ppermute(tall[-1], peer_axis, crops))]
    all_gather x3, waiting for transfers between devices: 166 us -> 98 us  [project(): full = lax.all_gather(piece, 'ctx', axis=0, tiled=True)]
    all_gather x1 -> x0, waiting for transfers between devices: 62 us -> none  [body(): lax.all_gather(w_out, 'ctx', axis=0, tiled=True)]
    ppermute x0 -> x7, starting transfers between devices: none -> 15.1 us  [the longest x3 9.23 us: plan_the_panels(): taken_in.append(jax.lax.ppermute(taken_in[-1], peer_axis, seen))]
    unnamed x13 -> x30, local copies, waits for them, and re-layouts: 9.79 us -> 24.4 us
  transfers between devices with their start and end apart: 5 -> 11, of which waited for: 4 -> 8; matrix products, arithmetic and copies ran while one was open for 9% -> 12% of each run, Pallas kernels for 0% -> 0%
where the time goes in v1:
time: 308 us
  waiting for transfers between devices  190 us (62%)
  blocking collectives  38.9 us (13%)
  local copies, waits for them, and re-layouts  29.2 us (9%)
  starting transfers between devices  18.3 us (6%)
  matrix products  15.8 us (5%)
  between operations  13.3 us (4%)
    all_gather x3, waiting for transfers between devices, project(): full = lax.all_gather(piece, 'ctx', axis=0, tiled=True)  98 us
    ppermute x4, waiting for transfers between devices, plan_the_panels(): tall.append(jax.lax.ppermute(tall[-1], peer_axis, crops))  78.3 us
    all_gather x1, blocking collectives, modal_long_conv(): states = lax.all_gather(end_state, 'ctx', axis=0, tiled=False)  31.8 us
    unnamed x30, local copies, waits for them, and re-layouts  24.4 us
    ppermute x3, waiting for transfers between devices, plan_the_panels(): taken_in.append(jax.lax.ppermute(taken_in[-1], peer_axis, seen))  11.6 us
    dot_general x3, matrix products, project(): out = jnp.dot(rows, full, preferred_element_type=jnp.float32)  9.24 us
    ppermute x3, starting transfers between devices, plan_the_panels(): taken_in.append(jax.lax.ppermute(taken_in[-1], peer_axis, seen))  9.23 us
    all_gather x1, blocking collectives, body(): features = lax.all_gather(gated, 'tp', axis=1, tiled=True)  7.15 us
  transfers between devices with their start and end apart: 11, of which 8 were waited for; matrix products, arithmetic and copies ran while one was open for 12% of the time, Pallas kernels for 0%

profile of v1, /device:TPU:0, one launch (start us, length us, event | category | flops | bytes accessed | tf_op | source)
XLA Modules:
  0.0 307.5 jit_solution(10907013143696413552)
XLA Ops:
  6.5 0.7 all-gather.7.cloned.1.call-update
  7.3 0.7 all-gather.9.cloned.1.call-update
  8.7 3.0 collective-permute-start.1
  11.8 16.8 %collective-permute-done.1 = bf16[256,1024]{1,0:T(8,128)(2,1)S(1)} collective-permute-done((bf16[256,1024]{1,0:T(8,128)(2,1)}, bf16[256,1024]{1,0:T(8,128)(2,1)S(1)}, u32[]{:S(2)}, u32[]{:S(2)}) %collective-permute-start.1) | collective-permute-done | bytes 524320 | tf_op jit(solution)/shard_map/ppermute | solution.py:13
  29.0 4.4 %collective-permute-start.5 = (bf16[256,1024]{1,0:T(8,128)(2,1)}, bf16[256,1024]{1,0:T(8,128)(2,1)S(1)}, u32[]{:S(2)}, u32[]{:S(2)}) collective-permute-start(bf16[256,1024]{1,0:T(8,128)(2,1)} %param.21), channel_id=1, source_target_pairs={{0,28},{4,0},{8,4},{12,8},{16,12},{20,16},{24,20},{28,24},{1,29},{... | collective-permute-start | bytes 1572872 | tf_op jit(solution)/shard_map/ppermute | solution.py:15
  33.3 21.8 %collective-permute-done.2 = bf16[256,1024]{1,0:T(8,128)(2,1)S(1)} collective-permute-done((bf16[256,1024]{1,0:T(8,128)(2,1)S(1)}, bf16[256,1024]{1,0:T(8,128)(2,1)S(1)}, u32[]{:S(2)}, u32[]{:S(2)}) %collective-permute-start.2) | collective-permute-done | bytes 524320 | tf_op jit(solution)/shard_map/ppermute | solution.py:13
  55.1 0.9 slice.62
  56.0 3.2 %collective-permute-start = (bf16[2,4096]{1,0:T(2,128)(2,1)S(1)}, bf16[2,4096]{1,0:T(2,128)(2,1)S(1)}, u32[]{:S(2)}, u32[]{:S(2)}) collective-permute-start(bf16[2,4096]{1,0:T(2,128)(2,1)S(1)} %slice.62), channel_id=1, source_target_pairs={{0,4},{4,8},{8,12},{12,16},{16,20},{20,24},{24,28},{1,5},{5,9},{9,... | collective-permute-start | bytes 49160 | tf_op jit(solution)/shard_map/ppermute | solution.py:67
  59.2 0.8 copy.12
  60.0 0.8 fusion.30
  60.8 2.9 collective-permute-start.6
  63.7 24.5 %collective-permute-done.3 = bf16[256,1024]{1,0:T(8,128)(2,1)S(1)} collective-permute-done((bf16[256,1024]{1,0:T(8,128)(2,1)S(1)}, bf16[256,1024]{1,0:T(8,128)(2,1)S(1)}, u32[]{:S(2)}, u32[]{:S(2)}) %collective-permute-start.3) | collective-permute-done | bytes 524320 | tf_op jit(solution)/shard_map/ppermute | solution.py:13
  88.2 2.5 collective-permute-start.4
  90.7 0.8 fusion.31
  91.5 0.8 fusion.32
  92.3 11.6 %collective-permute-done.6 = bf16[256,1024]{1,0:T(8,128)(2,1)S(1)} collective-permute-done((bf16[256,1024]{1,0:T(8,128)(2,1)S(1)}, bf16[256,1024]{1,0:T(8,128)(2,1)S(1)}, u32[]{:S(2)}, u32[]{:S(2)}) %collective-permute-start.6) | collective-permute-done | bytes 524320 | tf_op jit(solution)/shard_map/ppermute | solution.py:15
  103.9 2.0 collective-permute-start.7
  105.9 15.2 %collective-permute-done.4 = bf16[256,1024]{1,0:T(8,128)(2,1)S(1)} collective-permute-done((bf16[256,1024]{1,0:T(8,128)(2,1)S(1)}, bf16[256,1024]{1,0:T(8,128)(2,1)S(1)}, u32[]{:S(2)}, u32[]{:S(2)}) %collective-permute-start.4) | collective-permute-done | bytes 524320 | tf_op jit(solution)/shard_map/ppermute | solution.py:13
  121.1 0.8 constant_dynamic-update-slice_fusion.15
  121.9 0.8 constant_dynamic-update-slice_fusion.14
  122.8 0.9 constant_dynamic-update-slice_fusion.13
  123.6 0.8 constant_dynamic-update-slice_fusion.12
  124.5 0.8 constant_dynamic-update-slice_fusion.11
  125.3 0.8 constant_dynamic-update-slice_fusion.10
  126.2 0.8 constant_dynamic-update-slice_fusion.9
  127.0 0.8 constant_dynamic-update-slice_fusion.8
  127.8 0.8 constant_dynamic-update-slice_fusion.7
  128.7 0.8 constant_dynamic-update-slice_fusion.6
  129.5 0.9 constant_dynamic-update-slice_fusion.5
  130.4 0.8 constant_dynamic-update-slice_fusion.4
  131.2 0.8 constant_dynamic-update-slice_fusion.3
  132.0 0.8 constant_dynamic-update-slice_fusion.2
  132.9 0.8 constant_dynamic-update-slice_fusion.1
  133.7 0.9 constant_dynamic-update-slice_fusion
  134.6 1.6 all-gather.7.cloned.1.call-done
  136.2 3.3 %fusion.14 = f32[130,512]{1,0:T(8,128)S(1)} fusion(bf16[4096,512]{1,0:T(8,128)(2,1)} %all-gather.7.cloned.1.call-done, bf16[128,4096]{1,0:T(8,128)(2,1)} %param.11, bf16[2,4096]{1,0:T(2,128)(2,1)S(1)} %collective-permute-done), kind=kOutput, calls=%fused_computation.15 | convolution fusion | flops 547522560 | bytes 5525504 | tf_op jit(solution)/shard_map/dot_general | solution.py:72
  139.5 72.1 %all-gather.9.cloned.1.call-done = bf16[4096,512]{1,0:T(8,128)(2,1)} async-done(((bf16[512,512]{1,0:T(8,128)(2,1)}), bf16[4096,512]{1,0:T(8,128)(2,1)}) %all-gather.9.cloned.1.call-update) | async-done | bytes 4194320 | tf_op jit(solution)/shard_map/all_gather | solution.py:71
  211.6 3.0 fusion.13
  215.3 3.4 %copy.13 = f32[16,8,16,512]{3,1,2,0:T(8,128)S(1)} copy(f32[16,8,16,512]{3,2,1,0:T(8,128)S(1)} %bitcast.27) | data formatting | bytes 8388608
  218.8 2.9 fusion.4
  221.7 1.9 copy-done
  223.8 5.6 %copy.14 = f32[16,8,16,512]{3,2,1,0:T(8,128)S(1)} copy(f32[16,8,16,512]{3,1,2,0:T(8,128)} %bitcast.25) | data formatting | bytes 8388608
  229.4 31.8 %all-gather = f32[128,512]{1,0:T(8,128)S(1)} all-gather(f32[16,512]{1,0:T(8,128)S(1)} %get-tuple-element.6), channel_id=2, replica_groups=mesh['ctx'=8,'tp'=4] {'ctx'}, dimensions={0}, use_global_device_ids=true | all-gather | bytes 294912 | tf_op jit(solution)/shard_map/all_gather | solution.py:41
  261.4 1.5 fusion.1
  262.8 24.2 %all-gather.5.cloned.1.call-done = bf16[4096,512]{1,0:T(8,128)(2,1)} async-done(((bf16[512,512]{1,0:T(8,128)(2,1)}), bf16[4096,512]{1,0:T(8,128)(2,1)}) %all-gather.5.cloned.1.call-update) | async-done | bytes 4194320 | tf_op jit(solution)/shard_map/all_gather | solution.py:71
  287.1 3.0 fusion.15
  290.2 7.1 %all_gather.23 = bf16[128,2048]{1,0:T(8,128)(2,1)S(1)} all-gather(bf16[128,512]{1,0:T(8,128)(2,1)S(1)} %multiply_convert_fusion), channel_id=1, replica_groups=mesh['ctx'=8,'tp'=4] {'tp'}, dimensions={1}, use_global_device_ids=true | all-gather | bytes 655360 | tf_op jit(solution)/shard_map/all_gather | solution.py:85
  297.4 3.6 %fusion.10 = bf16[128,1024]{1,0:T(8,128)(2,1)} fusion(bf16[128,2048]{1,0:T(8,128)(2,1)S(1)} %all_gather.23, bf16[4096,1024]{1,0:T(8,128)(2,1)} %constant_dynamic-update-slice_fusion, s32[]{:T(128)S(6)} %select_n.19), kind=kOutput, calls=%fused_computation.11 | convolution fusion | flops 537001984 | bytes 4980740 | tf_op jit(solution)/shard_map/dot_general | solution.py:86
  (30 shorter events, 2.2 us)
Async XLA Ops:
  6.5 117.9 %copy-start.1 = (bf16[256,1024]{1,0:T(8,128)(2,1)S(1)}, bf16[256,1024]{1,0:T(8,128)(2,1)}, u32[]{:S(2)}) copy-start(bf16[256,1024]{1,0:T(8,128)(2,1)} %param.21) | copy-start | bytes 1572868
  6.5 129.7 %all-gather.7.cloned.1.call-start = ((), (), s32[]{:S(2)}) async-start(), calls=%async_computation.1 | async-start | bytes 4718592 | tf_op jit(solution)/shard_map/all_gather | solution.py:71
  7.3 204.4 %all-gather.9.cloned.1.call-start = ((), (), s32[]{:S(2)}) async-start(), calls=%async_computation.2 | async-start | bytes 4718592 | tf_op jit(solution)/shard_map/all_gather | solution.py:71
  8.0 279.1 %all-gather.5.cloned.1.call-start = ((), (), s32[]{:S(2)}) async-start(), calls=%async_computation | async-start | bytes 4718592 | tf_op jit(solution)/shard_map/all_gather | solution.py:71
  8.7 19.9 %collective-permute-start.1 = (bf16[256,1024]{1,0:T(8,128)(2,1)}, bf16[256,1024]{1,0:T(8,128)(2,1)S(1)}, u32[]{:S(2)}, u32[]{:S(2)}) collective-permute-start(bf16[256,1024]{1,0:T(8,128)(2,1)} %param.21), channel_id=1, source_target_pairs={{0,4},{4,8},{8,12},{12,16},{16,20},{20,24},{24,28},{28,0},{1,5},{5... | collective-permute-start | bytes 1572872 | tf_op jit(solution)/shard_map/ppermute | solution.py:13
  28.6 26.5 %collective-permute-start.2 = (bf16[256,1024]{1,0:T(8,128)(2,1)S(1)}, bf16[256,1024]{1,0:T(8,128)(2,1)S(1)}, u32[]{:S(2)}, u32[]{:S(2)}) collective-permute-start(bf16[256,1024]{1,0:T(8,128)(2,1)S(1)} %collective-permute-done.1), channel_id=1, source_target_pairs={{0,4},{4,8},{8,12},{12,16},{16,20},{20,24},{24,28},{28,0},{1,5},{5... | collective-permute-start | bytes 1572872 | tf_op jit(solution)/shard_map/ppermute | solution.py:13
  29.0 31.8 %collective-permute-start.5 = (bf16[256,1024]{1,0:T(8,128)(2,1)}, bf16[256,1024]{1,0:T(8,128)(2,1)S(1)}, u32[]{:S(2)}, u32[]{:S(2)}) collective-permute-start(bf16[256,1024]{1,0:T(8,128)(2,1)} %param.21), channel_id=1, source_target_pairs={{0,28},{4,0},{8,4},{12,8},{16,12},{20,16},{24,20},{28,24},{1,29},{... | collective-permute-start | bytes 1572872 | tf_op jit(solution)/shard_map/ppermute | solution.py:15
  55.1 33.1 %collective-permute-start.3 = (bf16[256,1024]{1,0:T(8,128)(2,1)S(1)}, bf16[256,1024]{1,0:T(8,128)(2,1)S(1)}, u32[]{:S(2)}, u32[]{:S(2)}) collective-permute-start(bf16[256,1024]{1,0:T(8,128)(2,1)S(1)} %collective-permute-done.2), channel_id=1, source_target_pairs={{0,4},{4,8},{8,12},{12,16},{16,20},{20,24},{24,28},{28,0},{1,5},{5... | collective-permute-start | bytes 1572872 | tf_op jit(solution)/shard_map/ppermute | solution.py:13
  56.0 78.6 %collective-permute-start = (bf16[2,4096]{1,0:T(2,128)(2,1)S(1)}, bf16[2,4096]{1,0:T(2,128)(2,1)S(1)}, u32[]{:S(2)}, u32[]{:S(2)}) collective-permute-start(bf16[2,4096]{1,0:T(2,128)(2,1)S(1)} %slice.62), channel_id=1, source_target_pairs={{0,4},{4,8},{8,12},{12,16},{16,20},{20,24},{24,28},{1,5},{5,9},{9,... | collective-permute-start | bytes 49160 | tf_op jit(solution)/shard_map/ppermute | solution.py:67
  60.8 43.1 %collective-permute-start.6 = (bf16[256,1024]{1,0:T(8,128)(2,1)S(1)}, bf16[256,1024]{1,0:T(8,128)(2,1)S(1)}, u32[]{:S(2)}, u32[]{:S(2)}) collective-permute-start(bf16[256,1024]{1,0:T(8,128)(2,1)S(1)} %collective-permute-done.5), channel_id=1, source_target_pairs={{0,28},{4,0},{8,4},{12,8},{16,12},{20,16},{24,20},{28,24},{1,29},{... | collective-permute-start | bytes 1572872 | tf_op jit(solution)/shard_map/ppermute | solution.py:15
  88.2 32.9 %collective-permute-start.4 = (bf16[256,1024]{1,0:T(8,128)(2,1)S(1)}, bf16[256,1024]{1,0:T(8,128)(2,1)S(1)}, u32[]{:S(2)}, u32[]{:S(2)}) collective-permute-start(bf16[256,1024]{1,0:T(8,128)(2,1)S(1)} %collective-permute-done.3), channel_id=1, source_target_pairs={{0,4},{4,8},{8,12},{12,16},{16,20},{20,24},{24,28},{28,0},{1,5},{5... | collective-permute-start | bytes 1572872 | tf_op jit(solution)/shard_map/ppermute | solution.py:13
  103.9 23.1 %collective-permute-start.7 = (bf16[256,1024]{1,0:T(8,128)(2,1)S(1)}, bf16[256,1024]{1,0:T(8,128)(2,1)S(1)}, u32[]{:S(2)}, u32[]{:S(2)}) collective-permute-start(bf16[256,1024]{1,0:T(8,128)(2,1)S(1)} %collective-permute-done.6), channel_id=1, source_target_pairs={{0,28},{4,0},{8,4},{12,8},{16,12},{20,16},{24,20},{28,24},{1,29},{... | collective-permute-start | bytes 1572872 | tf_op jit(solution)/shard_map/ppermute | solution.py:15
  132.9 78.8 %copy-start.5 = (bf16[128,4096]{1,0:T(8,128)(2,1)S(1)}, bf16[128,4096]{1,0:T(8,128)(2,1)}, u32[]{:S(2)}) copy-start(bf16[128,4096]{1,0:T(8,128)(2,1)} %param.11) | copy-start | bytes 3145732
  221.7 1.9 copy-start
  223.7 5.7 %copy-start.2 = (f32[16,512]{1,0:T(8,128)S(1)}, f32[16,512]{1,0:T(8,128)}, u32[]{:S(2)}) copy-start(f32[16,512]{1,0:T(8,128)} %param.18) | copy-start | bytes 98308
  223.7 5.7 %copy-start.3 = (f32[16,512]{1,0:T(8,128)S(1)}, f32[16,512]{1,0:T(8,128)}, u32[]{:S(2)}) copy-start(f32[16,512]{1,0:T(8,128)} %param.19) | copy-start | bytes 98308
  261.4 28.7 %copy-start.4 = (f32[512]{0:T(512)S(1)}, f32[512]{0:T(512)}, u32[]{:S(2)}) copy-start(f32[512]{0:T(512)} %param.20) | copy-start | bytes 6148
Sparse Core Ops, SparseCore 0:
  9.5 126.7 all-gather.6
  138.4 73.2 all-gather.8
  213.8 73.2 all-gather.4
